TPU v7x, 32 devices: a whole 2x2x4 slice. The times are simulated.
32 devices in a mesh: heads: 4 (over y, core), seq: 8 (over z, x).
Axes of the slice: x: 2, y: 2, z: 4, core: 2. Of those that a mesh axis runs over, the one named last changes fastest.
Arguments:
- hidden: bfloat16 [8, 256, 2048], P('seq', 'heads'), may hold values from -6 to 6
- norm_gain: bfloat16 [2048], replicated, may hold values from 0.099609375 to 1.8984375
- router_weight: bfloat16 [2048, 4], replicated, may hold values from -0.125 to 0.125
- att_experts: int32 [8, 256, 2], P('seq'), may hold values from 0 to 3, all different within a row
- q_weight: bfloat16 [4, 2048, 1024], P(None, None, 'heads'), may hold values from -0.125 to 0.125
- kv_weight: bfloat16 [2, 2048, 1024], P(None, None, 'heads'), may hold values from -0.125 to 0.125
- o_weight: bfloat16 [4, 1024, 2048], P(None, 'heads'), may hold values from -1 to 1
- kv_cache: bfloat16 [2, 128, 128, 1024], P(None, 'seq', None, 'heads'), may hold values from -200 to 200
- cached_blocks: int32 [8], replicated, may hold values from 1 to 32, 128 in all
- tail_trim: int32 [8], replicated, may hold values from 0 to 127
- block_pool: int32 [128], replicated, may hold values from 0 to 127, each once
Outputs:
- attn_out: bfloat16 [8, 256, 2048], P('seq', 'heads')
Inputs may be any that keep to these rules, and one draw needn't show every extreme that they name: `block_pool`: the cached_blocks sum to 128, so every block belongs to one request.
All inputs are finite; a program needn't handle non-finite values.
Results may differ from a plain program's by a relative error of at most 0.019.
The roundings to bfloat16 on the way count: a program that leaves them out, or rounds other values in their place, can miss the bound.
Values may be sent and summed in bfloat16 or wider, within the bound.
No kernel may reach another device: no remote copies, remote signals or barrier semaphores. Data moves between devices by JAX's collectives and lax.ppermute only.
A program may use at most 128 MiB of HBM per device.

v0:
```python
import jax
import jax.numpy as jnp
from jax import lax
from jax.sharding import PartitionSpec as P

HD = 128
NEG_FILL = -1e30


def rotate(values, positions):
    half_dim = values.shape[-1] // 2
    inverse = 10000.0 ** (-2.0 * jnp.arange(half_dim, dtype=jnp.float32) / values.shape[-1])
    angles = positions.astype(jnp.float32)[:, None] * inverse[None, :]
    target = (values.shape[0],) + (1,) * (values.ndim - 2) + (half_dim,)
    cosine = jnp.cos(angles).reshape(target)
    sine_part = jnp.sin(angles).reshape(target)
    leading_part = values[..., :half_dim]
    trailing_part = values[..., half_dim:]
    return jnp.concatenate(
        [
            leading_part * cosine - trailing_part * sine_part,
            trailing_part * cosine + leading_part * sine_part,
        ],
        axis=-1,
    )


def normalize(rows, norm_gain):
    wide_rows = rows.astype(jnp.float32)
    scaled = wide_rows * lax.rsqrt(jnp.mean(wide_rows * wide_rows, axis=-1, keepdims=True) + 1e-05)
    return (scaled * norm_gain.astype(jnp.float32)).astype(jnp.bfloat16)


def route(normed, router_weight, chosen):
    logits = jnp.dot(normed, router_weight, preferred_element_type=jnp.float32)
    experts_all = router_weight.shape[1]
    onehot = (chosen[:, :, None] == jnp.arange(experts_all, dtype=jnp.int32)[None, None, :]).astype(
        jnp.float32
    )
    picked = jnp.sum(onehot * logits[:, None, :], axis=-1)
    return (onehot, jax.nn.softmax(picked, axis=-1))


def per_device(
    hidden,
    norm_gain,
    router_weight,
    att_experts,
    q_weight,
    kv_weight,
    o_weight,
    kv_cache,
    cached_blocks,
    tail_trim,
    block_pool,
):
    head_count = lax.axis_size("heads")
    seq_rank = lax.axis_index("seq")
    block_size = kv_cache.shape[2]
    local_blocks = kv_cache.shape[1]
    local_heads = q_weight.shape[2] // HD
    scale_q = HD ** (-0.5)
    normed = normalize(hidden[0], norm_gain)
    gathered = lax.all_gather(normed, "heads", axis=0, tiled=True)
    new_count = gathered.shape[0]
    chosen = att_experts[0]
    cached_len = cached_blocks * block_size - tail_trim
    positions = cached_len[seq_rank] + jnp.arange(new_count, dtype=jnp.int32)
    onehot, gates = route(gathered, router_weight, chosen)
    every_q = jnp.einsum("nd,edc->nec", gathered, q_weight, preferred_element_type=jnp.float32)
    chosen_q = jnp.sum(onehot[:, :, :, None] * every_q[:, None, :, :], axis=2).reshape(
        new_count, 2, local_heads, HD
    )
    queries = rotate(chosen_q, positions).astype(jnp.bfloat16)
    fresh = jnp.einsum("nd,sdc->snc", gathered, kv_weight, preferred_element_type=jnp.float32)
    new_keys = rotate(fresh[0].reshape(new_count, local_heads, HD), positions).astype(jnp.bfloat16)
    new_values = fresh[1].reshape(new_count, local_heads, HD).astype(jnp.bfloat16)
    all_queries = lax.all_gather(queries[None], "seq", axis=0, tiled=True)
    request_count = all_queries.shape[0]
    pool_size = block_pool.shape[0]
    global_ids = seq_rank * local_blocks + jnp.arange(local_blocks, dtype=jnp.int32)
    matches = block_pool[None, :] == global_ids[:, None]
    slot_of = jnp.sum(
        jnp.where(matches, jnp.arange(pool_size, dtype=jnp.int32)[None, :], 0), axis=1
    )
    starts = jnp.cumsum(cached_blocks) - cached_blocks
    owner = jnp.sum((starts[None, :] <= slot_of[:, None]).astype(jnp.int32), axis=1) - 1
    ordinal = slot_of - starts[owner]
    stat_shape = (request_count, new_count, 2, local_heads)
    initial = (
        jnp.full(stat_shape, NEG_FILL, jnp.float32),
        jnp.zeros(stat_shape, jnp.float32),
        jnp.zeros(stat_shape + (HD,), jnp.float32),
    )

    def visit(carry, block):
        best, totals, accum = carry
        request = owner[block]
        query_rows = lax.dynamic_index_in_dim(all_queries, request, 0, keepdims=False)
        pair_kv = lax.dynamic_index_in_dim(kv_cache, block, 1, keepdims=False)
        keys_here = pair_kv[0].reshape(block_size, local_heads, HD)
        values_here = pair_kv[1].reshape(block_size, local_heads, HD)
        scores = (
            jnp.einsum("nkhc,thc->nkht", query_rows, keys_here, preferred_element_type=jnp.float32)
            * scale_q
        )
        key_pos = ordinal[block] * block_size + jnp.arange(block_size, dtype=jnp.int32)
        scores = jnp.where((key_pos < cached_len[request])[None, None, None, :], scores, NEG_FILL)
        old_best = lax.dynamic_index_in_dim(best, request, 0, keepdims=False)
        new_best = jnp.maximum(old_best, jnp.max(scores, axis=-1))
        weights = jnp.exp(scores - new_best[..., None])
        rescale = jnp.exp(old_best - new_best)
        new_total = lax.dynamic_index_in_dim(
            totals, request, 0, keepdims=False
        ) * rescale + jnp.sum(weights, axis=-1)
        product = jnp.einsum(
            "nkht,thc->nkhc",
            weights.astype(jnp.bfloat16),
            values_here,
            preferred_element_type=jnp.float32,
        )
        new_accum = (
            lax.dynamic_index_in_dim(accum, request, 0, keepdims=False) * rescale[..., None]
            + product
        )
        best = lax.dynamic_update_index_in_dim(best, new_best, request, 0)
        totals = lax.dynamic_update_index_in_dim(totals, new_total, request, 0)
        accum = lax.dynamic_update_index_in_dim(accum, new_accum, request, 0)
        return ((best, totals, accum), None)

    scanned = lax.scan(visit, initial, jnp.arange(local_blocks, dtype=jnp.int32))
    best, totals, accum = scanned[0]
    self_scores = (
        jnp.einsum("nkhc,thc->nkht", queries, new_keys, preferred_element_type=jnp.float32)
        * scale_q
    )
    causal = (
        jnp.arange(new_count, dtype=jnp.int32)[None, :]
        <= jnp.arange(new_count, dtype=jnp.int32)[:, None]
    )
    self_scores = jnp.where(causal[:, None, None, :], self_scores, NEG_FILL)
    self_best = jnp.max(self_scores, axis=-1)
    self_weights = jnp.exp(self_scores - self_best[..., None])
    self_total = jnp.sum(self_weights, axis=-1)
    self_accum = jnp.einsum(
        "nkht,thc->nkhc",
        self_weights.astype(jnp.bfloat16),
        new_values,
        preferred_element_type=jnp.float32,
    )
    global_best = lax.pmax(best.astype(jnp.bfloat16), "seq").astype(best.dtype)
    factor = jnp.exp(best - global_best)
    cache_accum, cache_total = (
        lax.psum_scatter(
            (accum * factor[..., None]).astype(jnp.bfloat16), "seq", scatter_dimension=0, tiled=True
        ).astype(jnp.float32),
        lax.psum_scatter(
            (totals * factor).astype(jnp.bfloat16), "seq", scatter_dimension=0, tiled=True
        ).astype(jnp.float32),
    )
    cache_best = lax.dynamic_index_in_dim(global_best, seq_rank, 0, keepdims=True)
    peak = jnp.maximum(cache_best[0], self_best)
    cache_share = jnp.exp(cache_best[0] - peak)
    self_share = jnp.exp(self_best - peak)
    numerator = cache_accum[0] * cache_share[..., None] + self_accum * self_share[..., None]
    denominator = cache_total[0] * cache_share + self_total * self_share
    attended = (
        (numerator / denominator[..., None])
        .astype(jnp.bfloat16)
        .reshape(new_count, 2, local_heads * HD)
    )
    rows_each = new_count // head_count
    output = jnp.zeros((rows_each * lax.axis_size("heads"), o_weight.shape[2]), jnp.float32)
    for expert in range(o_weight.shape[0]):
        weight_expert = jnp.sum(onehot[:, :, expert] * gates, axis=1)
        picked = jnp.where(
            chosen[:, 0:1] == expert,
            attended[:, 0],
            jnp.where(chosen[:, 1:2] == expert, attended[:, 1], jnp.zeros_like(attended[:, 0])),
        )
        output = output + weight_expert[:, None] * jnp.dot(
            picked, o_weight[expert], preferred_element_type=jnp.float32
        )
    summed = lax.psum_scatter(
        output.astype(jnp.bfloat16), "heads", scatter_dimension=0, tiled=True
    ).astype(jnp.float32)
    return summed[None].astype(jnp.bfloat16)


def solution(mesh):
    return jax.shard_map(
        per_device,
        mesh=mesh,
        in_specs=(
            P("seq", "heads", None),
            P(),
            P(),
            P("seq", None, None),
            P(None, None, "heads"),
            P(None, None, "heads"),
            P(None, "heads", None),
            P(None, "seq", None, "heads"),
            P(),
            P(),
            P(),
        ),
        out_specs=P("seq", "heads", None),
        check_vma=False,
    )
```

profile of v0, /device:TPU:0, one launch (start us, length us, event | category | flops | bytes accessed | tf_op | source)
XLA Modules:
  0.0 434.2 jit_solution(16295591473125909563)
XLA Ops:
  8.5 1.8 fusion.37
  15.1 14.8 %all-gather.3.cloned.1.call-done = bf16[256,2048]{1,0:T(8,128)(2,1)} async-done(((bf16[64,2048]{1,0:T(8,128)(2,1)}), bf16[256,2048]{1,0:T(8,128)(2,1)}) %all-gather.3.cloned.1.call-update) | async-done | bytes 1048592 | tf_op jit(solution)/shard_map/all_gather | solution.py:64
  29.9 3.8 fusion.27
  38.4 48.4 %all-gather.5.cloned.1.call-done = bf16[8,256,2,2,128]{4,1,3,2,0:T(8,128)(2,1)} async-done(((bf16[1,256,2,2,128]{4,1,3,2,0:T(8,128)(2,1)}), bf16[8,256,2,2,128]{4,1,3,2,0:T(8,128)(2,1)}) %all-gather.5.cloned.1.call-update) | async-done | bytes 2097168 | tf_op jit(solution)/shard_map/all_gather | solution.py:78
  86.8 2.4 broadcast_in_dim.133
  89.2 202.3 %while.14 = (s32[]{:T(128)}, f32[8,256,2,2]{1,2,3,0:T(2,128)S(1)}, f32[8,256,2,2]{1,2,3,0:T(2,128)S(1)}, f32[8,256,2,2,128]{1,4,2,3,0:T(8,128)}, s32[16]{0:T(128...) while((s32[]{:T(128)}, f32[8,256,2,2]{1,2,3,0:T(2,128)S(1)}, ...), condition=%wide.region_12.13_spmd, body=%wide.region_9.12_spmd.sunk | while | flops 68292872 | bytes 4649549 | solution.py:131
  98.2 1.2 fusion.122
  161.4 1.2 fusion.122
  199.4 1.2 fusion.122
  212.0 1.2 fusion.122
  224.6 1.2 fusion.122
  275.2 1.2 fusion.122
  291.5 34.7 %pmax.7 = bf16[8,256,2,2]{1,2,3,0:T(2,128)(2,1)S(1)} all-reduce(bf16[8,256,2,2]{1,2,3,0:T(2,128)(2,1)S(1)} %convert_element_type.81), channel_id=1, replica_groups=mesh['heads'=4,'seq'=8] {'seq'}, use_global_device_ids=true, to_apply=%region_13.14 | all-reduce | flops 8192 | bytes 32768 | tf_op jit(solution)/shard_map/pmax | solution.py:151
  326.8 4.0 multiply_convert_fusion
  330.9 1.3 dynamic-slice
  332.3 1.4 compare_reduce_fusion.1
  336.3 1.6 fusion.103
  338.7 1.4 fusion.102
  340.3 33.7 %all-reduce = bf16[8,256,2,2]{1,2,3,0:T(2,128)(2,1)S(1)} all-reduce(bf16[8,256,2,2]{1,2,3,0:T(2,128)(2,1)} %get-tuple-element.139), channel_id=3, replica_groups=mesh['heads'=4,'seq'=8] {'seq'}, use_global_device_ids=true, to_apply=%region_16.17.clone | all-reduce | flops 8192 | bytes 32768
  374.5 22.9 %reduce-scatter.3.cloned.1.call-done = bf16[1,256,2,2,128]{1,4,2,3,0:T(8,128)(2,1)} async-done(((bf16[8,256,2,2,128]{1,4,2,3,0:T(8,128)(2,1)}), bf16[1,256,2,2,128]{1,4,2,3,0:T(8,128)(2,1)}) %reduce-scatter.3.cloned.1.call-update) | async-done | bytes 262160 | tf_op jit(solution)/shard_map/reduce_scatter | solution.py:154
  397.5 1.5 fusion.21
  399.0 1.7 convolution_multiply_fusion.4
  402.1 1.5 fusion.15
  403.6 24.0 %reduce-scatter.5.cloned.1.call-done = bf16[64,2048]{1,0:T(8,128)(2,1)} async-done(((bf16[256,2048]{1,0:T(8,128)(2,1)}), bf16[64,2048]{1,0:T(8,128)(2,1)}) %reduce-scatter.5.cloned.1.call-update) | async-done | bytes 262160 | tf_op jit(solution)/shard_map/reduce_scatter | solution.py:184
  (320 shorter events, 136.3 us)
Async XLA Ops:
  6.5 327.8 %copy-start = (bf16[2,2048,256]{2,1,0:T(8,128)(2,1)S(1)}, bf16[2,2048,256]{2,1,0:T(8,128)(2,1)}, u32[]{:S(2)}) copy-start(bf16[2,2048,256]{2,1,0:T(8,128)(2,1)} %param.18) | copy-start | bytes 6291460
  6.5 23.4 %all-gather.3.cloned.1.call-start = ((), (), s32[]{:S(2)}) async-start(), calls=%async_computation.2 | async-start | bytes 1310720 | tf_op jit(solution)/shard_map/all_gather | solution.py:64
  10.3 76.5 %all-gather.5.cloned.1.call-start = ((), (), s32[]{:S(2)}) async-start(), calls=%async_computation.3 | async-start | bytes 2359296 | tf_op jit(solution)/shard_map/all_gather | solution.py:78
  11.1 2.2 copy-start.5
  34.4 2.9 copy-start.21
  35.7 0.7 copy-start.2
  37.3 360.1 %reduce-scatter.3.cloned.1.call-start = ((), (), s32[]{:S(2)}) async-start(), calls=%async_computation.4 | async-start | bytes 2359296 | tf_op jit(solution)/shard_map/reduce_scatter | solution.py:154
  330.9 3.4 copy-start.4
  330.9 96.7 %reduce-scatter.5.cloned.1.call-start = ((), (), s32[]{:S(2)}) async-start(), calls=%async_computation.5 | async-start | bytes 1310720 | tf_op jit(solution)/shard_map/reduce_scatter | solution.py:184
  335.2 1.0 copy-start.8
  335.2 2.6 copy-start.7
  335.3 2.7 copy-start.6
  335.3 3.3 copy-start.3
  340.2 58.8 %copy-start.11 = (f32[256]{0:T(256)S(1)}, f32[256]{0:T(256)}, u32[]{:S(2)}) copy-start(f32[256]{0:T(256)} %get-tuple-element.105) | copy-start | bytes 3076
  340.2 58.8 %copy-start.17 = (pred[256]{0:T(512)(128)(4,1)S(1)}, pred[256]{0:T(512)(128)(4,1)}, u32[]{:S(2)}) copy-start(pred[256]{0:T(512)(128)(4,1)} %get-tuple-element.112) | copy-start | bytes 772
  340.2 58.8 %copy-start.18 = (pred[256]{0:T(512)(128)(4,1)S(1)}, pred[256]{0:T(512)(128)(4,1)}, u32[]{:S(2)}) copy-start(pred[256]{0:T(512)(128)(4,1)} %get-tuple-element.113) | copy-start | bytes 772
  397.5 3.3 copy-start.1
  398.9 1.8 copy-start.10
  399.0 1.8 copy-start.15
  399.0 1.8 copy-start.16
  400.8 0.7 copy-start.9
  400.8 0.7 copy-start.13
  401.4 0.7 copy-start.19
  401.4 0.7 copy-start.20
  (2 other events, 1.3 us)
Sparse Core Ops, SparseCore 0:
  10.4 19.4 all-gather.2
  37.4 49.2 all-gather.4
  331.0 66.3 reduce-scatter.2
  403.7 23.8 reduce-scatter.4
where the time goes:
time: 438 us; the launch traced here: 434 us
  waiting for transfers between devices  110 us (25%)
  local copies, waits for them, and re-layouts  84.8 us (19%)
  loops' own time  76 us (17%)
  blocking collectives  68.3 us (16%)
  matrix products  49.9 us (11%)
  other arithmetic  31.2 us (7%)
  between operations  13.6 us (3%)
    another operation x1, loops' own time, per_device(): lax.scan(visit, initial, jnp.arange(local_blocks, dtype=jnp.int32))  76 us
    all_gather x1, waiting for transfers between devices, per_device(): all_queries = lax.all_gather(queries[None], 'seq', axis=0, tiled=True)  48.4 us
    pmax x1, blocking collectives, per_device(): global_best = lax.pmax(best.astype(jnp.bfloat16), 'seq').astype(best.dtype)  34.7 us
    unnamed x1, blocking collectives  33.7 us
    reduce_scatter x1, waiting for transfers between devices, per_device(): lax.psum_scatter(output.astype(jnp.bfloat16), 'heads', scatter_dimension=...  24 us
    reduce_scatter x1, waiting for transfers between devices, per_device(): lax.psum_scatter((accum * factor[..., None]).astype(jnp.bfloat16), 'seq',...  22.9 us
    dot_general x16, matrix products, visit(): jnp.einsum('nkhc,thc->nkht', query_rows, keys_here, preferred_element_typ...  19.8 us
    dynamic_slice x16, local copies, waits for them, and re-layouts, visit(): lax.dynamic_index_in_dim(accum, request, 0, keepdims=False)  17.3 us
  transfers between devices with their start and end apart: 4, of which 4 were waited for; matrix products, arithmetic and copies ran while one was open for 4% of the time, Pallas kernels for 0%

commit v1 on v0

--- a/solution.py
+++ b/solution.py
@@ -75,7 +75,12 @@
     fresh = jnp.einsum("nd,sdc->snc", gathered, kv_weight, preferred_element_type=jnp.float32)
     new_keys = rotate(fresh[0].reshape(new_count, local_heads, HD), positions).astype(jnp.bfloat16)
     new_values = fresh[1].reshape(new_count, local_heads, HD).astype(jnp.bfloat16)
-    all_queries = lax.all_gather(queries[None], "seq", axis=0, tiled=True)
+    ring = [queries[None]]
+    for hop in range(7):
+        ring.append(lax.ppermute(ring[-1], "seq", [(dev, (dev + 1) % 8) for dev in range(8)]))
+    all_queries = jnp.roll(
+        jnp.concatenate(ring[::-1], axis=0), (lax.axis_index("seq") + 1) * ring[0].shape[0], axis=0
+    )
     request_count = all_queries.shape[0]
     pool_size = block_pool.shape[0]
     global_ids = seq_rank * local_blocks + jnp.arange(local_blocks, dtype=jnp.int32)

time: 438 us -> 457 us (1.043)
  waiting for transfers between devices: 110 us -> 124 us
  local copies, waits for them, and re-layouts: 84.8 us -> 91.7 us
    ppermute x0 -> x7, waiting for transfers between devices: none -> 65.9 us  [per_device(): lax.ppermute(ring[-1], 'seq', [(dev, (dev + 1) % 8) for dev in range(8)])]
    all_gather x1 -> x0, waiting for transfers between devices: 48.4 us -> none  [per_device(): all_queries = lax.all_gather(queries[None], 'seq', axis=0, tiled=True)]
    unnamed x49 -> x59, local copies, waits for them, and re-layouts: 3.06 us -> 12.8 us
  transfers between devices with their start and end apart: 4 -> 10, of which waited for: 4 -> 10; matrix products, arithmetic and copies ran while one was open for 4% -> 3% of each run, Pallas kernels for 0% -> 0%
where the time goes in v1:
time: 457 us; the launch traced here: 453 us
  waiting for transfers between devices  124 us (27%)
  local copies, waits for them, and re-layouts  91.7 us (20%)
  loops' own time  73.3 us (16%)
  blocking collectives  66.6 us (15%)
  matrix products  51.5 us (11%)
  other arithmetic  30.5 us (7%)
  between operations  13.7 us (3%)
    another operation x1, loops' own time, per_device(): lax.scan(visit, initial, jnp.arange(local_blocks, dtype=jnp.int32))  73.3 us
    ppermute x7, waiting for transfers between devices, per_device(): lax.ppermute(ring[-1], 'seq', [(dev, (dev + 1) % 8) for dev in range(8)])  65.9 us
    unnamed x1, blocking collectives  33.6 us
    pmax x1, blocking collectives, per_device(): global_best = lax.pmax(best.astype(jnp.bfloat16), 'seq').astype(best.dtype)  33 us
    reduce_scatter x1, waiting for transfers between devices, per_device(): lax.psum_scatter(output.astype(jnp.bfloat16), 'heads', scatter_dimension=...  24 us
    dot_general x16, matrix products, visit(): jnp.einsum('nkhc,thc->nkht', query_rows, keys_here, preferred_element_typ...  19.8 us
    reduce_scatter x1, waiting for transfers between devices, per_device(): lax.psum_scatter((accum * factor[..., None]).astype(jnp.bfloat16), 'seq',...  19 us
    dynamic_slice x16, local copies, waits for them, and re-layouts, visit(): lax.dynamic_index_in_dim(accum, request, 0, keepdims=False)  17.3 us
  transfers between devices with their start and end apart: 10, of which 10 were waited for; matrix products, arithmetic and copies ran while one was open for 3% of the time, Pallas kernels for 0%

profile of v1, /device:TPU:0, one launch (start us, length us, event | category | flops | bytes accessed | tf_op | source)
XLA Modules:
  0.0 453.4 jit_solution(16411925639068010212)
XLA Ops:
  8.5 1.8 fusion.40
  14.5 15.4 %all-gather.2.cloned.1.call-done = bf16[256,2048]{1,0:T(8,128)(2,1)} async-done(((bf16[64,2048]{1,0:T(8,128)(2,1)}), bf16[256,2048]{1,0:T(8,128)(2,1)}) %all-gather.2.cloned.1.call-update) | async-done | bytes 1048592 | tf_op jit(solution)/shard_map/all_gather | solution.py:64
  29.9 3.8 fusion.30
  36.9 1.5 collective-permute-start
  38.4 9.7 %collective-permute-done = bf16[1,256,2,2,128]{4,1,2,3,0:T(8,128)(2,1)S(1)} collective-permute-done((bf16[1,256,2,2,128]{4,1,2,3,0:T(8,128)(2,1)S(1)}, bf16[1,256,2,2,128]{4,1,2,3,0:T(8,128)(2,1)S(1)}, u32[]{:S(2)}, u32[]{:S(2)}) %collective-permute-start) | collective-permute-done | bytes 262176 | tf_op jit(solution)/shard_map/ppermute | solution.py:80
  48.0 10.3 %collective-permute-done.1 = bf16[1,256,2,2,128]{4,1,2,3,0:T(8,128)(2,1)S(1)} collective-permute-done((bf16[1,256,2,2,128]{4,1,2,3,0:T(8,128)(2,1)S(1)}, bf16[1,256,2,2,128]{4,1,2,3,0:T(8,128)(2,1)S(1)}, u32[]{:S(2)}, u32[]{:S(2)}) %collective-permute-start.1) | collective-permute-done | bytes 262176 | tf_op jit(solution)/shard_map/ppermute | solution.py:80
  58.4 9.4 %collective-permute-done.2 = bf16[1,256,2,2,128]{4,1,2,3,0:T(8,128)(2,1)S(1)} collective-permute-done((bf16[1,256,2,2,128]{4,1,2,3,0:T(8,128)(2,1)S(1)}, bf16[1,256,2,2,128]{4,1,2,3,0:T(8,128)(2,1)S(1)}, u32[]{:S(2)}, u32[]{:S(2)}) %collective-permute-start.2) | collective-permute-done | bytes 262176 | tf_op jit(solution)/shard_map/ppermute | solution.py:80
  68.5 9.2 %collective-permute-done.3 = bf16[1,256,2,2,128]{4,1,2,3,0:T(8,128)(2,1)} collective-permute-done((bf16[1,256,2,2,128]{4,1,2,3,0:T(8,128)(2,1)S(1)}, bf16[1,256,2,2,128]{4,1,2,3,0:T(8,128)(2,1)}, u32[]{:S(2)}, u32[]{:S(2)}) %collective-permute-start.3) | collective-permute-done | bytes 262176 | tf_op jit(solution)/shard_map/ppermute | solution.py:80
  77.8 9.2 %collective-permute-done.4 = bf16[1,256,2,2,128]{4,1,2,3,0:T(8,128)(2,1)} collective-permute-done((bf16[1,256,2,2,128]{4,1,2,3,0:T(8,128)(2,1)}, bf16[1,256,2,2,128]{4,1,2,3,0:T(8,128)(2,1)}, u32[]{:S(2)}, u32[]{:S(2)}) %collective-permute-start.4) | collective-permute-done | bytes 262176 | tf_op jit(solution)/shard_map/ppermute | solution.py:80
  87.1 9.5 %collective-permute-done.5 = bf16[1,256,2,2,128]{4,1,2,3,0:T(8,128)(2,1)} collective-permute-done((bf16[1,256,2,2,128]{4,1,2,3,0:T(8,128)(2,1)}, bf16[1,256,2,2,128]{4,1,2,3,0:T(8,128)(2,1)}, u32[]{:S(2)}, u32[]{:S(2)}) %collective-permute-start.5) | collective-permute-done | bytes 262176 | tf_op jit(solution)/shard_map/ppermute | solution.py:80
  97.3 8.7 %collective-permute-done.6 = bf16[1,256,2,2,128]{4,1,2,3,0:T(8,128)(2,1)} collective-permute-done((bf16[1,256,2,2,128]{4,1,2,3,0:T(8,128)(2,1)}, bf16[1,256,2,2,128]{4,1,2,3,0:T(8,128)(2,1)}, u32[]{:S(2)}, u32[]{:S(2)}) %collective-permute-start.6) | collective-permute-done | bytes 262176 | tf_op jit(solution)/shard_map/ppermute | solution.py:80
  115.5 1.5 constant_dynamic-slice_fusion.4
  117.0 2.4 broadcast_in_dim.133
  119.4 195.5 %while.14 = (s32[]{:T(128)}, f32[8,256,2,2]{1,2,3,0:T(2,128)S(1)}, f32[8,256,2,2]{1,2,3,0:T(2,128)S(1)}, f32[8,256,2,2,128]{1,4,2,3,0:T(8,128)}, s32[16]{0:T(128...) while((s32[]{:T(128)}, f32[8,256,2,2]{1,2,3,0:T(2,128)S(1)}, ...), condition=%wide.region_12.13_spmd, body=%wide.region_9.12_spmd.sunk | while | flops 68292872 | bytes 4649549 | solution.py:136
  315.0 33.0 %pmax.7 = bf16[8,256,2,2]{1,2,3,0:T(2,128)(2,1)S(1)} all-reduce(bf16[8,256,2,2]{1,2,3,0:T(2,128)(2,1)S(1)} %convert_element_type.81), channel_id=1, replica_groups=mesh['heads'=4,'seq'=8] {'seq'}, use_global_device_ids=true, to_apply=%region_13.14 | all-reduce | flops 8192 | bytes 32768 | tf_op jit(solution)/shard_map/pmax | solution.py:156
  348.6 4.0 multiply_convert_fusion
  354.7 2.2 convolution_bitcast_fusion.2
  357.8 1.6 fusion.106
  363.4 33.6 %all-reduce = bf16[8,256,2,2]{1,2,3,0:T(2,128)(2,1)S(1)} all-reduce(bf16[8,256,2,2]{1,2,3,0:T(2,128)(2,1)} %get-tuple-element.139), channel_id=3, replica_groups=mesh['heads'=4,'seq'=8] {'seq'}, use_global_device_ids=true, to_apply=%region_16.17.clone | all-reduce | flops 8192 | bytes 32768
  397.7 19.0 %reduce-scatter.3.cloned.1.call-done = bf16[1,256,2,2,128]{1,4,2,3,0:T(8,128)(2,1)} async-done(((bf16[8,256,2,2,128]{1,4,2,3,0:T(8,128)(2,1)}), bf16[1,256,2,2,128]{1,4,2,3,0:T(8,128)(2,1)}) %reduce-scatter.3.cloned.1.call-update) | async-done | bytes 262160 | tf_op jit(solution)/shard_map/reduce_scatter | solution.py:159
  416.7 1.7 fusion.24
  418.5 1.7 convolution_multiply_fusion.4
  421.3 1.5 fusion.18
  422.8 24.0 %reduce-scatter.5.cloned.1.call-done = bf16[64,2048]{1,0:T(8,128)(2,1)} async-done(((bf16[256,2048]{1,0:T(8,128)(2,1)}), bf16[64,2048]{1,0:T(8,128)(2,1)}) %reduce-scatter.5.cloned.1.call-update) | async-done | bytes 262160 | tf_op jit(solution)/shard_map/reduce_scatter | solution.py:189
  (343 shorter events, 151.7 us)
Async XLA Ops:
  6.5 348.1 %copy-start = (bf16[2,2048,256]{2,1,0:T(8,128)(2,1)S(1)}, bf16[2,2048,256]{2,1,0:T(8,128)(2,1)}, u32[]{:S(2)}) copy-start(bf16[2,2048,256]{2,1,0:T(8,128)(2,1)} %param.18) | copy-start | bytes 6291460
  6.5 23.4 %all-gather.2.cloned.1.call-start = ((), (), s32[]{:S(2)}) async-start(), calls=%async_computation.2 | async-start | bytes 1310720 | tf_op jit(solution)/shard_map/all_gather | solution.py:64
  10.3 406.4 %reduce-scatter.3.cloned.1.call-start = ((), (), s32[]{:S(2)}) async-start(), calls=%async_computation.3 | async-start | bytes 2359296 | tf_op jit(solution)/shard_map/reduce_scatter | solution.py:159
  33.7 44.0 %copy-start.18 = (s32[128]{0:T(128)S(1)}, s32[128]{0:T(128)}, u32[]{:S(2)}) copy-start(s32[128]{0:T(128)} %param.23) | copy-start | bytes 1540
  36.9 11.2 %collective-permute-start = (bf16[1,256,2,2,128]{4,1,2,3,0:T(8,128)(2,1)S(1)}, bf16[1,256,2,2,128]{4,1,2,3,0:T(8,128)(2,1)S(1)}, u32[]{:S(2)}, u32[]{:S(2)}) collective-permute-start(bf16[1,256,2,2,128]{4,1,2,3,0:T(8,128)(2,1)S(1)} %pad_maximum_fusion), channel_id=1, source_target_pairs={{0,1},{1,2},{2,3},{3,4},{4,5},{5,6},{6,7},{7,0},{8,9},{9,10},{10,1... | collective-permute-start | bytes 786440 | tf_op jit(solution)/shard_map/ppermute | solution.py:80
  48.0 10.3 %collective-permute-start.1 = (bf16[1,256,2,2,128]{4,1,2,3,0:T(8,128)(2,1)S(1)}, bf16[1,256,2,2,128]{4,1,2,3,0:T(8,128)(2,1)S(1)}, u32[]{:S(2)}, u32[]{:S(2)}) collective-permute-start(bf16[1,256,2,2,128]{4,1,2,3,0:T(8,128)(2,1)S(1)} %collective-permute-done), channel_id=1, source_target_pairs={{0,1},{1,2},{2,3},{3,4},{4,5},{5,6},{6,7},{7,0},{8,9},{9,10},{10,1... | collective-permute-start | bytes 786440 | tf_op jit(solution)/shard_map/ppermute | solution.py:80
  58.4 9.4 %collective-permute-start.2 = (bf16[1,256,2,2,128]{4,1,2,3,0:T(8,128)(2,1)S(1)}, bf16[1,256,2,2,128]{4,1,2,3,0:T(8,128)(2,1)S(1)}, u32[]{:S(2)}, u32[]{:S(2)}) collective-permute-start(bf16[1,256,2,2,128]{4,1,2,3,0:T(8,128)(2,1)S(1)} %collective-permute-done.1), channel_id=1, source_target_pairs={{0,1},{1,2},{2,3},{3,4},{4,5},{5,6},{6,7},{7,0},{8,9},{9,10},{10,1... | collective-permute-start | bytes 786440 | tf_op jit(solution)/shard_map/ppermute | solution.py:80
  68.5 9.2 %collective-permute-start.3 = (bf16[1,256,2,2,128]{4,1,2,3,0:T(8,128)(2,1)S(1)}, bf16[1,256,2,2,128]{4,1,2,3,0:T(8,128)(2,1)}, u32[]{:S(2)}, u32[]{:S(2)}) collective-permute-start(bf16[1,256,2,2,128]{4,1,2,3,0:T(8,128)(2,1)S(1)} %collective-permute-done.2), channel_id=1, source_target_pairs={{0,1},{1,2},{2,3},{3,4},{4,5},{5,6},{6,7},{7,0},{8,9},{9,10},{10,1... | collective-permute-start | bytes 786440 | tf_op jit(solution)/shard_map/ppermute | solution.py:80
  77.6 9.4 %collective-permute-start.4 = (bf16[1,256,2,2,128]{4,1,2,3,0:T(8,128)(2,1)}, bf16[1,256,2,2,128]{4,1,2,3,0:T(8,128)(2,1)}, u32[]{:S(2)}, u32[]{:S(2)}) collective-permute-start(bf16[1,256,2,2,128]{4,1,2,3,0:T(8,128)(2,1)} %collective-permute-done.3), channel_id=1, source_target_pairs={{0,1},{1,2},{2,3},{3,4},{4,5},{5,6},{6,7},{7,0},{8,9},{9,10},{10,1... | collective-permute-start | bytes 786440 | tf_op jit(solution)/shard_map/ppermute | solution.py:80
  87.0 9.6 %collective-permute-start.5 = (bf16[1,256,2,2,128]{4,1,2,3,0:T(8,128)(2,1)}, bf16[1,256,2,2,128]{4,1,2,3,0:T(8,128)(2,1)}, u32[]{:S(2)}, u32[]{:S(2)}) collective-permute-start(bf16[1,256,2,2,128]{4,1,2,3,0:T(8,128)(2,1)} %collective-permute-done.4), channel_id=1, source_target_pairs={{0,1},{1,2},{2,3},{3,4},{4,5},{5,6},{6,7},{7,0},{8,9},{9,10},{10,1... | collective-permute-start | bytes 786440 | tf_op jit(solution)/shard_map/ppermute | solution.py:80
  96.6 9.4 %collective-permute-start.6 = (bf16[1,256,2,2,128]{4,1,2,3,0:T(8,128)(2,1)}, bf16[1,256,2,2,128]{4,1,2,3,0:T(8,128)(2,1)}, u32[]{:S(2)}, u32[]{:S(2)}) collective-permute-start(bf16[1,256,2,2,128]{4,1,2,3,0:T(8,128)(2,1)} %collective-permute-done.5), channel_id=1, source_target_pairs={{0,1},{1,2},{2,3},{3,4},{4,5},{5,6},{6,7},{7,0},{8,9},{9,10},{10,1... | collective-permute-start | bytes 786440 | tf_op jit(solution)/shard_map/ppermute | solution.py:80
  97.3 17.9 %copy-start.4 = (bf16[1,256,2,2,128]{4,1,2,3,0:T(8,128)(2,1)S(1)}, bf16[1,256,2,2,128]{4,1,2,3,0:T(8,128)(2,1)}, u32[]{:S(2)}) copy-start(bf16[1,256,2,2,128]{4,1,2,3,0:T(8,128)(2,1)} %copy-done.3) | copy-start | bytes 786436
  348.0 4.7 %copy-start.5 = (bf16[8,256,2,2]{1,2,3,0:T(2,128)(2,1)}, bf16[8,256,2,2]{1,2,3,0:T(2,128)(2,1)S(1)}, u32[]{:S(2)}) copy-start(bf16[8,256,2,2]{1,2,3,0:T(2,128)(2,1)S(1)} %pmax.7) | copy-start | bytes 49156
  348.6 4.1 copy-start.19
  348.6 4.8 %copy-start.7 = (s32[1,256,2]{1,2,0:T(2,128)S(1)}, s32[1,256,2]{1,2,0:T(2,128)}, u32[]{:S(2)}) copy-start(s32[1,256,2]{1,2,0:T(2,128)} %param.16) | copy-start | bytes 6148
  352.7 94.1 %reduce-scatter.5.cloned.1.call-start = ((), (), s32[]{:S(2)}) async-start(), calls=%async_computation.4 | async-start | bytes 1310720 | tf_op jit(solution)/shard_map/reduce_scatter | solution.py:189
  357.8 58.9 %copy-start.6 = (bf16[1,256,256]{1,2,0:T(8,128)(2,1)S(1)}, bf16[1,256,256]{1,2,0:T(8,128)(2,1)}, u32[]{:S(2)}) copy-start(bf16[1,256,256]{1,2,0:T(8,128)(2,1)} %slice.186) | copy-start | bytes 393220
  360.2 58.3 %copy-start.10 = (f32[256]{0:T(256)S(1)}, f32[256]{0:T(256)}, u32[]{:S(2)}) copy-start(f32[256]{0:T(256)} %get-tuple-element.105) | copy-start | bytes 3076
  361.5 58.7 %copy-start.9 = (f32[256]{0:T(256)S(1)}, f32[256]{0:T(256)}, u32[]{:S(2)}) copy-start(f32[256]{0:T(256)} %get-tuple-element.104) | copy-start | bytes 3076
  361.5 58.7 %copy-start.14 = (pred[256]{0:T(512)(128)(4,1)S(1)}, pred[256]{0:T(512)(128)(4,1)}, u32[]{:S(2)}) copy-start(pred[256]{0:T(512)(128)(4,1)} %get-tuple-element.107) | copy-start | bytes 772
  361.5 58.7 %copy-start.15 = (pred[256]{0:T(512)(128)(4,1)S(1)}, pred[256]{0:T(512)(128)(4,1)}, u32[]{:S(2)}) copy-start(pred[256]{0:T(512)(128)(4,1)} %get-tuple-element.109) | copy-start | bytes 772
  416.7 3.6 copy-start.1
  418.5 2.3 copy-start.8
  418.5 2.3 copy-start.12
  (6 other events, 7.1 us)
Sparse Core Ops, SparseCore 0:
  10.4 19.4 all-gather.1
  352.8 63.8 reduce-scatter.2
  422.9 23.8 reduce-scatter.4
